TPU v7x, 256 devices: a whole 4x4x8 slice. The times are simulated.
256 devices in a mesh: dom: 16 (over x, y), slab: 16 (over z, core).
Axes of the slice: x: 4, y: 4, z: 8, core: 2. Of those that a mesh axis runs over, the one named last changes fastest.
Arguments:
- images: bfloat16 [4096, 8192], P(('dom', 'slab')), may hold values from -64 to 64
- defocus: bfloat16 [4096], P(('dom', 'slab')), may hold values from 20 to 60
- inv_noise: float32 [4096], replicated, may hold values from 0.01 to 0.04
- slices: bfloat16 [128, 8192], P('slab'), may hold values from -5 to 5
- lists: int32 [4096, 32], P(('dom', 'slab')), may hold values from 0 to 127, as said below
- counts: int32 [4096], P(('dom', 'slab')), may hold values from 0 to 32, as said below
Outputs:
- peak_weight: float32 [4096], P(('dom', 'slab'))
- data_sum: float32 [128, 8192], P('slab', 'dom')
- weight_sum: float32 [128, 4096], P('slab', 'dom')
Inputs may be any that keep to these rules, and one draw needn't show every extreme that they name: `lists`: the 32 entries of a row are different orientations. `counts`: 0 marks a particle left out of this pass; a particle that takes part has 2 or more significant orientations.
All inputs are finite; a program needn't handle non-finite values.
Results may differ from a plain program's by a relative error of at most 0.009.
Values may be sent and summed in bfloat16 or wider, within the bound.
No kernel may reach another device: no remote copies, remote signals or barrier semaphores. Data moves between devices by JAX's collectives and lax.ppermute only.
A program may use at most 128 MiB of HBM per device.

v0:
```python
import math
import jax
import jax.numpy as jnp
from jax import lax
from jax.sharding import PartitionSpec as P

SIDE = 64
COEF = 4096
TRANS = 25
SENTINEL = -1e30
HIGHEST = lax.Precision.HIGHEST


def frequency_grid():
    position = jnp.arange(COEF, dtype=jnp.int32)
    freq_x = (position // SIDE - SIDE // 2).astype(jnp.float32)
    freq_y = (position % SIDE - SIDE // 2).astype(jnp.float32)
    return (freq_x, freq_y)


def shift_tables(freq_x, freq_y):
    edge = math.isqrt(TRANS)
    half = edge // 2
    offsets = jnp.arange(TRANS, dtype=jnp.int32)
    shift_x = (offsets // edge - half).astype(jnp.float32)
    shift_y = (offsets % edge - half).astype(jnp.float32)
    angle = (
        2.0
        * jnp.pi
        * (shift_x[:, None] * freq_x[None, :] + shift_y[:, None] * freq_y[None, :])
        / SIDE
    )
    return (jnp.cos(angle), jnp.sin(angle))


def rotate_rows(values, cosine, sine):
    real_part = values[:, None, :COEF]
    imag_part = values[:, None, COEF:]
    turned = jnp.concatenate(
        (real_part * cosine - imag_part * sine, real_part * sine + imag_part * cosine), axis=-1
    )
    return turned.reshape(values.shape[0] * TRANS, 2 * COEF)


def significance(lists, counts, offset, number):
    orient_ids = offset + jnp.arange(number, dtype=jnp.int32)
    slot_live = jnp.arange(lists.shape[1], dtype=jnp.int32)[None, :] < counts[:, None]
    hits = (lists[:, :, None] == orient_ids[None, None, :]) & slot_live[:, :, None]
    return jnp.any(hits, axis=1)


def expectation(
    images,
    defocus,
    lists,
    counts,
    inv_noise,
    slices,
    offset,
    tile,
    reduce_highest,
    reduce_normalizer,
):
    row_count = images.shape[0]
    orient_count = slices.shape[0]
    freq_x, freq_y = frequency_grid()
    cosine, sine = shift_tables(freq_x, freq_y)
    radius = (freq_x * freq_x + freq_y * freq_y) / (SIDE * SIDE)
    ordering = jnp.argsort((counts <= 0).astype(jnp.int32), stable=True)
    sorted_images = jnp.take(images, ordering, axis=0)
    sorted_defocus = jnp.take(defocus, ordering, axis=0)
    sorted_lists = jnp.take(lists, ordering, axis=0)
    sorted_counts = jnp.take(counts, ordering, axis=0)
    alive = sorted_counts > 0
    live_tiles = (jnp.sum(alive.astype(jnp.int32)) + tile - 1) // tile
    ctf = -jnp.sin(jnp.pi * sorted_defocus.astype(jnp.float32)[:, None] * radius[None, :] + 0.1)
    real_part = sorted_images[:, :COEF].astype(jnp.float32)
    imag_part = sorted_images[:, COEF:].astype(jnp.float32)
    weighted = jnp.concatenate(
        (inv_noise * ctf * real_part, inv_noise * ctf * imag_part), axis=-1
    ).astype(jnp.bfloat16)
    image_half = jnp.concatenate((ctf * real_part, ctf * imag_part), axis=-1).astype(jnp.bfloat16)
    quad_half = -0.5 * inv_noise * ctf * ctf
    quadratic = jnp.concatenate((quad_half, quad_half), axis=-1).astype(jnp.bfloat16)
    slices_wide = slices.astype(jnp.float32)
    squares = (slices_wide * slices_wide).astype(jnp.bfloat16)
    energy = lax.dot_general(
        quadratic, squares, (((1,), (1,)), ((), ())), preferred_element_type=jnp.float32
    )
    mask = significance(sorted_lists, sorted_counts, offset, orient_count)

    def score_step(tile_step, buffer):
        rows_weighted = weighted.astype(jnp.float32)
        linear = lax.dot_general(
            rotate_rows(rows_weighted, cosine, sine),
            slices_wide,
            (((1,), (1,)), ((), ())),
            precision=HIGHEST,
        )
        linear = linear.reshape(tile, TRANS, orient_count)
        score = jnp.where(mask[:, None, :], linear + energy[:, None, :], SENTINEL)
        return score

    start_buffer = jnp.full((row_count, TRANS, orient_count), SENTINEL, jnp.float32)
    buffer = lax.fori_loop(0, live_tiles, score_step, start_buffer)
    highest = reduce_highest(jnp.max(buffer, axis=(1, 2)))
    highest = jnp.where(alive, highest, 0.0)
    expo = jnp.where(buffer > 0.5 * SENTINEL, jnp.exp(buffer - highest[:, None, None]), 0.0)
    normalizer = reduce_normalizer(jnp.sum(expo, axis=(1, 2)))
    normalizer = jnp.where(alive, normalizer, 1.0)
    posterior_half = (expo / normalizer[:, None, None]).astype(jnp.bfloat16)
    peak_sorted = jnp.where(alive, 1.0 / normalizer, 0.0)
    peak_values = jnp.zeros((row_count,), jnp.float32).at[ordering].set(peak_sorted)

    def sum_step(tile_step, total):
        return total + lax.dot_general(
            posterior_half.astype(jnp.float32).reshape(tile * TRANS, orient_count),
            rotate_rows(image_half.astype(jnp.float32), cosine, sine),
            (((0,), (0,)), ((), ())),
            precision=HIGHEST,
        )

    data_sum = lax.fori_loop(
        0, live_tiles, sum_step, jnp.zeros((orient_count, 2 * COEF), jnp.float32)
    )
    per_orient = jnp.sum(posterior_half.astype(jnp.float32), axis=1)
    ctf_half = (ctf * ctf).astype(jnp.bfloat16).astype(jnp.float32)
    weight_sum = lax.dot_general(per_orient, ctf_half, (((0,), (0,)), ((), ())), precision=HIGHEST)
    return (peak_values, data_sum, weight_sum)


def keep_values(values):
    return values


def shards(images, defocus, inv_noise, slices, lists, counts):
    whole_slices = lax.all_gather(slices, "slab", axis=0, tiled=True)
    peak_weight, data_sum, weight_sum = expectation(
        images, defocus, lists, counts, inv_noise, whole_slices, 0, 16, keep_values, keep_values
    )
    data_sum, weight_sum = (
        lax.psum_scatter(data_sum, "slab", scatter_dimension=0, tiled=True),
        lax.psum_scatter(weight_sum, "slab", scatter_dimension=0, tiled=True),
    )
    data_sum, weight_sum = (
        lax.psum_scatter(data_sum, "dom", scatter_dimension=1, tiled=True),
        lax.psum_scatter(weight_sum, "dom", scatter_dimension=1, tiled=True),
    )
    return (peak_weight, data_sum, weight_sum)


def solution(mesh):
    placed = (
        P(("dom", "slab"), None),
        P(("dom", "slab")),
        P(),
        P("slab", None),
        P(("dom", "slab"), None),
        P(("dom", "slab")),
    )
    return jax.shard_map(
        shards,
        mesh=mesh,
        in_specs=placed,
        out_specs=(P(("dom", "slab")), P("slab", "dom"), P("slab", "dom")),
        check_vma=False,
    )
```

profile of v0, /device:TPU:2, one launch (start us, length us, event | category | flops | bytes accessed | tf_op | source)
XLA Modules:
  0.0 366.6 jit_solution(13582859348225433491)
XLA Ops:
  7.2 0.0 copy-start
  7.2 0.0 all-gather.2.cloned.1.call-start
  7.2 0.7 all-gather.2.cloned.1.call-update
  7.9 0.0 reduce-scatter.9.cloned.1.call-start
  8.0 0.7 compare_convert_fusion
  8.6 1.2 sort.17
  9.9 1.3 gather_fusion
  11.2 1.3 gather_fusion.2
  12.6 0.6 convert_reduce_fusion.1
  13.9 0.1 iota_compare_fusion.1
  14.0 1.3 gather_fusion.1
  15.2 0.1 broadcast_select_fusion.1
  15.3 0.7 broadcast_multiply_fusion
  16.0 0.7 gather_fusion.3
  16.7 0.1 broadcast_select_fusion
  16.9 0.2 fusion.36
  17.1 1.8 fusion.25
  18.8 0.1 maximum_convert_fusion
  18.9 1.9 fusion.24
  20.9 7.0 %multiply_subtract_fusion.1 = (f32[16,25,4096]{2,1,0:T(8,128)}, f32[16,25,4096]{2,1,0:T(8,128)}) fusion(f32[25,4096]{1,0:T(8,128)S(1)} %get-tuple-element.288, f32[16,4096]{1,0:T(8,128)S(1)} %get-tuple-element.282, f32[25,4096]{1,0:T(8,128)S(1)} %get-tuple-element.287, f32[16,4096]{1,0:T(8,128)S(1)} %get-tuple-element.281), kind=kLoop, calls=%fused_computation.25 | loop fusion | flops 9830400 | bytes 14450688 | tf_op jit(solution)/shard_map/while/body/sub | solution.py:40
  27.9 24.3 %all-gather.2.cloned.1.call-done = bf16[128,8192]{1,0:T(8,128)(2,1)} async-done(((bf16[8,8192]{1,0:T(8,128)(2,1)}), bf16[128,8192]{1,0:T(8,128)(2,1)}) %all-gather.2.cloned.1.call-update) | async-done | bytes 2097168 | tf_op jit(solution)/shard_map/all_gather | solution.py:137
  52.2 2.2 fusion.21
  54.5 12.4 %fusion.17 = f32[16,25,128]{2,1,0:T(8,128)S(1)} fusion(f32[16,25,4096]{2,1,0:T(8,128)} %get-tuple-element.280, f32[16,25,4096]{2,1,0:T(8,128)} %get-tuple-element.279, bf16[128,8192]{1,0:T(8,128)(2,1)} %all-gather.2.cloned.1.call-done), kind=kOutput, calls=%fused_computation.20 | convolution fusion | flops 5036441600 | bytes 15409152 | tf_op jit(solution)/shard_map/while/body/dot_general | solution.py:94
  66.9 0.7 broadcast_in_dim.63
  67.6 0.7 while.25
  67.6 0.7 add_select_fusion.3
  68.3 1.2 reduce_max.9
  69.5 1.3 fusion.37
  70.8 1.1 convert_reduce_fusion
  71.9 3.0 fusion.38
  74.9 0.0 reduce-scatter.9.cloned.1.call-update
  75.0 0.0 reduce-scatter.5.cloned.1.call-start
  75.0 2.2 broadcast_in_dim.94
  77.2 29.6 %while.26 = (s32[]{:T(128)}, f32[128,8192]{0,1:T(8,128)}, s32[]{:T(128)}, bf16[16,8192]{1,0:T(8,128)(2,1)S(1)}, bf16[16,25,128]{2,1,0:T(8,128)(2,1)S(1)}, /*inde...) while((s32[]{:T(128)}, f32[128,8192]{0,1:T(8,128)}, ...), condition=%wide.region_9.10_spmd.clone.clone.clone, body=%wide.region_8.9_spmd.clone.clone.clone.sunk | while | flops 5047730176 | bytes 37949740 | solution.py:123
  77.3 1.9 fusion.73
  79.2 7.0 %multiply_subtract_fusion.3 = (f32[16,25,4096]{2,1,0:T(8,128)}, f32[16,25,4096]{2,1,0:T(8,128)}) fusion(f32[25,4096]{1,0:T(8,128)S(1)} %get-tuple-element.396, f32[16,4096]{1,0:T(8,128)S(1)} %get-tuple-element.397, f32[25,4096]{1,0:T(8,128)S(1)} %get-tuple-element.398, f32[16,4096]{1,0:T(8,128)S(1)} %get-tuple-element.399), kind=kLoop, calls=%fused_computation.15.clone.1 | loop fusion | flops 9830400 | bytes 14450688 | tf_op jit(solution)/shard_map/while/body/sub | solution.py:40
  86.2 20.6 %fusion.75 = f32[128,8192]{0,1:T(8,128)} fusion(f32[128,8192]{0,1:T(8,128)} %get-tuple-element.434, bf16[16,25,128]{2,1,0:T(8,128)(2,1)S(1)} %get-tuple-element.447, f32[16,25,4096]{2,1,0:T(8,128)} %get-tuple-element.400, f32[16,25,4096]{2,1,0:T(8,128)} %get-tuple-element.401), kind=kOutput, calls=%fused_computation.13.clone.1 | convolution fusion | flops 5037490176 | bytes 21598208 | tf_op jit(solution)/shard_map/while/body/dot_general | solution.py:116
  106.8 5.7 %copy.11 = f32[128,8192]{1,0:T(8,128)} copy(f32[128,8192]{0,1:T(8,128)} %get-tuple-element.146) | data formatting | bytes 8388608 | tf_op jit(solution)/shard_map/while | solution.py:123
  112.5 0.0 reduce-scatter.5.cloned.1.call-update
  112.5 0.0 reduce-scatter.11.cloned.1.call-start
  112.5 20.9 %reduce-scatter.9.cloned.1.call-done = f32[8,4096]{1,0:T(8,128)} async-done(((f32[128,4096]{1,0:T(8,128)}), f32[8,4096]{1,0:T(8,128)}) %reduce-scatter.9.cloned.1.call-update) | async-done | bytes 131088 | tf_op jit(solution)/shard_map/reduce_scatter | solution.py:143
  133.5 0.0 reduce-scatter.11.cloned.1.call-update
  133.5 0.0 reduce-scatter.7.cloned.1.call-start
  133.5 64.5 %reduce-scatter.5.cloned.1.call-done = f32[8,8192]{1,0:T(8,128)} async-done(((f32[128,8192]{1,0:T(8,128)}), f32[8,8192]{1,0:T(8,128)}) %reduce-scatter.5.cloned.1.call-update) | async-done | bytes 262160 | tf_op jit(solution)/shard_map/reduce_scatter | solution.py:142
  198.0 0.0 reduce-scatter.7.cloned.1.call-update
  198.1 1.1 scatter_custom_fusion
  199.2 79.3 %reduce-scatter.11.cloned.1.call-done = f32[8,256]{1,0:T(8,128)} async-done(((f32[8,4096]{1,0:T(8,128)}), f32[8,256]{1,0:T(8,128)}) %reduce-scatter.11.cloned.1.call-update) | async-done | bytes 8208 | tf_op jit(solution)/shard_map/reduce_scatter | solution.py:147
  278.5 81.6 %reduce-scatter.7.cloned.1.call-done = f32[8,512]{1,0:T(8,128)} async-done(((f32[8,8192]{1,0:T(8,128)}), f32[8,512]{1,0:T(8,128)}) %reduce-scatter.7.cloned.1.call-update) | async-done | bytes 16400 | tf_op jit(solution)/shard_map/reduce_scatter | solution.py:146
  (12 shorter events, 0.1 us)
Async XLA Ops:
  7.2 8.9 %copy-start = (bf16[16,8192]{1,0:T(8,128)(2,1)S(1)}, bf16[16,8192]{1,0:T(8,128)(2,1)}, u32[]{:S(2)}) copy-start(bf16[16,8192]{1,0:T(8,128)(2,1)} %param.10) | copy-start | bytes 786436
  7.2 45.1 %all-gather.2.cloned.1.call-start = ((), (), s32[]{:S(2)}) async-start(), calls=%async_computation.4 | async-start | bytes 2228224 | tf_op jit(solution)/shard_map/all_gather | solution.py:137
  7.9 125.6 %reduce-scatter.9.cloned.1.call-start = ((), (), s32[]{:S(2)}) async-start(), calls=%async_computation.7 | async-start | bytes 2228224 | tf_op jit(solution)/shard_map/reduce_scatter | solution.py:143
  75.0 123.1 %reduce-scatter.5.cloned.1.call-start = ((), (), s32[]{:S(2)}) async-start(), calls=%async_computation.5 | async-start | bytes 4456448 | tf_op jit(solution)/shard_map/reduce_scatter | solution.py:142
  112.5 166.0 %reduce-scatter.11.cloned.1.call-start = ((), (), s32[]{:S(2)}) async-start(), calls=%async_computation.8 | async-start | bytes 139264 | tf_op jit(solution)/shard_map/reduce_scatter | solution.py:147
  133.5 226.6 %reduce-scatter.7.cloned.1.call-start = ((), (), s32[]{:S(2)}) async-start(), calls=%async_computation.6 | async-start | bytes 278528 | tf_op jit(solution)/shard_map/reduce_scatter | solution.py:146
Sparse Core Ops, SparseCore 0:
  9.8 42.3 all-gather.1
  75.1 58.3 reduce-scatter.8
  136.0 61.9 reduce-scatter.4
  201.9 76.4 reduce-scatter.10
  282.4 77.6 reduce-scatter.6
where the time goes:
time: 367 us
  waiting for transfers between devices  271 us (74%)
  matrix products  38.3 us (10%)
  other arithmetic  27.8 us (8%)
  between operations  14.6 us (4%)
  local copies, waits for them, and re-layouts  14.4 us (4%)
    reduce_scatter x1, waiting for transfers between devices, shards(): lax.psum_scatter(data_sum, 'dom', scatter_dimension=1, tiled=True)  81.6 us
    reduce_scatter x1, waiting for transfers between devices, shards(): lax.psum_scatter(weight_sum, 'dom', scatter_dimension=1, tiled=True)  79.3 us
    reduce_scatter x1, waiting for transfers between devices, shards(): lax.psum_scatter(data_sum, 'slab', scatter_dimension=0, tiled=True)  64.5 us
    all_gather x1, waiting for transfers between devices, shards(): whole_slices = lax.all_gather(slices, 'slab', axis=0, tiled=True)  24.3 us
    reduce_scatter x1, waiting for transfers between devices, shards(): lax.psum_scatter(weight_sum, 'slab', scatter_dimension=0, tiled=True)  20.9 us
    dot_general x1, matrix products, sum_step(): lax.dot_general(posterior_half.astype(jnp.float32).reshape(tile * TRANS,...  20.6 us
    sub x2, other arithmetic, rotate_rows(): real_part * cosine - imag_part * sine  14.1 us
    dot_general x1, matrix products, score_step(): lax.dot_general(rotate_rows(rows_weighted, cosine, sine), slices_wide, ((...  12.4 us
  transfers between devices with their start and end apart: 5, of which 5 were waited for; matrix products, arithmetic and copies ran while one was open for 16% of the time, Pallas kernels for 0%

commit v1 on v0

--- a/solution.py
+++ b/solution.py
@@ -3,6 +3,7 @@
 import jax.numpy as jnp
 from jax import lax
 from jax.sharding import PartitionSpec as P
+from jax.lax import all_to_all, axis_size
 
 SIDE = 64
 COEF = 4096
@@ -134,7 +135,9 @@
 
 
 def shards(images, defocus, inv_noise, slices, lists, counts):
-    whole_slices = lax.all_gather(slices, "slab", axis=0, tiled=True)
+    u1 = jnp.stack([slices for _ in range(axis_size("slab"))], axis=0)
+    v_now = all_to_all(u1, "slab", split_axis=0, concat_axis=0)
+    whole_slices = jnp.concatenate(v_now, axis=0)
     peak_weight, data_sum, weight_sum = expectation(
         images, defocus, lists, counts, inv_noise, whole_slices, 0, 16, keep_values, keep_values
     )

time: 367 us -> 381 us (1.038)
  starting transfers between devices: 0.2 us -> 8.73 us
  waiting for transfers between devices: 271 us -> 277 us
    all_to_all x0 -> x1, waiting for transfers between devices: none -> 30 us  [shards(): v_now = all_to_all(u1, 'slab', split_axis=0, concat_axis=0)]
    all_gather x1 -> x0, waiting for transfers between devices: 24.3 us -> none  [shards(): whole_slices = lax.all_gather(slices, 'slab', axis=0, tiled=True)]
    all_to_all x0 -> x1, starting transfers between devices: none -> 8.57 us  [shards(): v_now = all_to_all(u1, 'slab', split_axis=0, concat_axis=0)]
  transfers between devices with their start and end apart: 5 -> 5, of which waited for: 5 -> 5; matrix products, arithmetic and copies ran while one was open for 16% -> 15% of each run, Pallas kernels for 0% -> 0%
where the time goes in v1:
time: 381 us
  waiting for transfers between devices  277 us (73%)
  matrix products  36.1 us (9%)
  other arithmetic  27 us (7%)
  local copies, waits for them, and re-layouts  16.9 us (4%)
  between operations  14.6 us (4%)
  starting transfers between devices  8.73 us (2%)
    reduce_scatter x1, waiting for transfers between devices, shards(): lax.psum_scatter(data_sum, 'dom', scatter_dimension=1, tiled=True)  81.7 us
    reduce_scatter x1, waiting for transfers between devices, shards(): lax.psum_scatter(weight_sum, 'dom', scatter_dimension=1, tiled=True)  79.3 us
    reduce_scatter x1, waiting for transfers between devices, shards(): lax.psum_scatter(data_sum, 'slab', scatter_dimension=0, tiled=True)  64.7 us
    all_to_all x1, waiting for transfers between devices, shards(): v_now = all_to_all(u1, 'slab', split_axis=0, concat_axis=0)  30 us
    reduce_scatter x1, waiting for transfers between devices, shards(): lax.psum_scatter(weight_sum, 'slab', scatter_dimension=0, tiled=True)  21.6 us
    dot_general x1, matrix products, sum_step(): lax.dot_general(posterior_half.astype(jnp.float32).reshape(tile * TRANS,...  20.5 us
    sub x2, other arithmetic, rotate_rows(): real_part * cosine - imag_part * sine  14 us
    dot_general x1, matrix products, score_step(): lax.dot_general(rotate_rows(rows_weighted, cosine, sine), slices_wide, ((...  11.9 us
  transfers between devices with their start and end apart: 5, of which 5 were waited for; matrix products, arithmetic and copies ran while one was open for 15% of the time, Pallas kernels for 0%

profile of v1, /device:TPU:2, one launch (start us, length us, event | category | flops | bytes accessed | tf_op | source)
XLA Modules:
  0.0 380.7 jit_solution(3970014028350118632)
XLA Ops:
  7.2 0.0 copy-start
  7.2 2.5 stack.2
  9.7 8.6 %all-to-all-start = ((bf16[16,8,8192]{2,1,0:T(8,128)(2,1)}), bf16[16,8,8192]{2,1,0:T(8,128)(2,1)S(1)}, u32[]{:S(2)}, u32[]{:S(2)}) async-start(bf16[16,8,8192]{2,1,0:T(8,128)(2,1)} %stack.2), calls=%async_computation | async-start | bytes 4194304 | tf_op jit(solution)/shard_map/all_to_all | solution.py:139
  18.3 0.0 reduce-scatter.9.cloned.1.call-start
  18.3 0.7 compare_convert_fusion
  19.0 1.2 sort.17
  20.3 1.3 gather_fusion
  21.6 1.3 gather_fusion.2
  22.9 0.6 convert_reduce_fusion.1
  24.3 0.1 iota_compare_fusion.1
  24.3 1.3 gather_fusion.1
  25.6 0.1 broadcast_select_fusion.1
  25.7 0.7 broadcast_multiply_fusion
  26.4 0.7 gather_fusion.3
  27.1 0.1 broadcast_select_fusion
  27.2 0.2 fusion.37
  27.4 1.0 fusion.26
  28.5 0.1 maximum_convert_fusion
  28.6 1.9 fusion.25
  30.5 6.9 %multiply_subtract_fusion.1 = (f32[16,25,4096]{2,1,0:T(8,128)}, f32[16,25,4096]{2,1,0:T(8,128)}) fusion(f32[25,4096]{1,0:T(8,128)S(1)} %get-tuple-element.288, f32[16,4096]{1,0:T(8,128)S(1)} %get-tuple-element.282, f32[25,4096]{1,0:T(8,128)S(1)} %get-tuple-element.287, f32[16,4096]{1,0:T(8,128)S(1)} %get-tuple-element.281), kind=kLoop, calls=%fused_computation.25 | loop fusion | flops 9830400 | bytes 14450688 | tf_op jit(solution)/shard_map/while/body/sub | solution.py:41
  37.5 30.0 %all-to-all-done = bf16[16,8,8192]{2,1,0:T(8,128)(2,1)S(1)} async-done(((bf16[16,8,8192]{2,1,0:T(8,128)(2,1)}), bf16[16,8,8192]{2,1,0:T(8,128)(2,1)S(1)}, u32[]{:S(2)}, u32[]{:S(2)}) %all-to-all-start) | async-done | bytes 2097184 | tf_op jit(solution)/shard_map/all_to_all | solution.py:139
  67.5 0.6 fusion.21
  68.1 11.9 %fusion.17 = f32[16,25,128]{2,1,0:T(8,128)S(1)} fusion(f32[16,25,4096]{2,1,0:T(8,128)} %get-tuple-element.280, f32[16,25,4096]{2,1,0:T(8,128)} %get-tuple-element.279, bf16[16,8,8192]{2,1,0:T(8,128)(2,1)S(1)} %all-to-all-done), kind=kOutput, calls=%fused_computation.20 | convolution fusion | flops 5036441600 | bytes 15409152 | tf_op jit(solution)/shard_map/while/body/dot_general | solution.py:95
  80.0 0.7 broadcast_in_dim.63
  80.8 0.7 while.25
  80.8 0.7 add_select_fusion.3
  81.5 1.2 reduce_max.9
  82.7 1.3 fusion.38
  83.9 1.1 convert_reduce_fusion
  85.1 3.0 fusion.39
  88.1 0.0 reduce-scatter.9.cloned.1.call-update
  88.1 0.0 reduce-scatter.5.cloned.1.call-start
  88.2 2.2 broadcast_in_dim.94
  90.4 29.6 %while.26 = (s32[]{:T(128)}, f32[128,8192]{0,1:T(8,128)}, s32[]{:T(128)}, bf16[16,8192]{1,0:T(8,128)(2,1)S(1)}, bf16[16,25,128]{2,1,0:T(8,128)(2,1)S(1)}, /*inde...) while((s32[]{:T(128)}, f32[128,8192]{0,1:T(8,128)}, ...), condition=%wide.region_9.10_spmd.clone.clone.clone, body=%wide.region_8.9_spmd.clone.clone.clone.sunk | while | flops 5047730176 | bytes 37949740 | solution.py:124
  90.4 1.9 fusion.74
  92.3 7.0 %multiply_subtract_fusion.3 = (f32[16,25,4096]{2,1,0:T(8,128)}, f32[16,25,4096]{2,1,0:T(8,128)}) fusion(f32[25,4096]{1,0:T(8,128)S(1)} %get-tuple-element.396, f32[16,4096]{1,0:T(8,128)S(1)} %get-tuple-element.397, f32[25,4096]{1,0:T(8,128)S(1)} %get-tuple-element.398, f32[16,4096]{1,0:T(8,128)S(1)} %get-tuple-element.399), kind=kLoop, calls=%fused_computation.15.clone.1 | loop fusion | flops 9830400 | bytes 14450688 | tf_op jit(solution)/shard_map/while/body/sub | solution.py:41
  99.4 20.5 %fusion.76 = f32[128,8192]{0,1:T(8,128)} fusion(f32[128,8192]{0,1:T(8,128)} %get-tuple-element.434, bf16[16,25,128]{2,1,0:T(8,128)(2,1)S(1)} %get-tuple-element.447, f32[16,25,4096]{2,1,0:T(8,128)} %get-tuple-element.400, f32[16,25,4096]{2,1,0:T(8,128)} %get-tuple-element.401), kind=kOutput, calls=%fused_computation.13.clone.1 | convolution fusion | flops 5037490176 | bytes 21598208 | tf_op jit(solution)/shard_map/while/body/dot_general | solution.py:117
  119.9 5.6 %copy.11 = f32[128,8192]{1,0:T(8,128)} copy(f32[128,8192]{0,1:T(8,128)} %get-tuple-element.146) | data formatting | bytes 8388608 | tf_op jit(solution)/shard_map/while | solution.py:124
  125.6 0.0 reduce-scatter.5.cloned.1.call-update
  125.6 0.0 reduce-scatter.11.cloned.1.call-start
  125.6 21.6 %reduce-scatter.9.cloned.1.call-done = f32[8,4096]{1,0:T(8,128)} async-done(((f32[128,4096]{1,0:T(8,128)}), f32[8,4096]{1,0:T(8,128)}) %reduce-scatter.9.cloned.1.call-update) | async-done | bytes 131088 | tf_op jit(solution)/shard_map/reduce_scatter | solution.py:146
  147.3 0.0 reduce-scatter.11.cloned.1.call-update
  147.3 0.0 reduce-scatter.7.cloned.1.call-start
  147.3 64.7 %reduce-scatter.5.cloned.1.call-done = f32[8,8192]{1,0:T(8,128)} async-done(((f32[128,8192]{1,0:T(8,128)}), f32[8,8192]{1,0:T(8,128)}) %reduce-scatter.5.cloned.1.call-update) | async-done | bytes 262160 | tf_op jit(solution)/shard_map/reduce_scatter | solution.py:145
  212.0 0.0 reduce-scatter.7.cloned.1.call-update
  212.1 1.1 scatter_custom_fusion
  213.2 79.3 %reduce-scatter.11.cloned.1.call-done = f32[8,256]{1,0:T(8,128)} async-done(((f32[8,4096]{1,0:T(8,128)}), f32[8,256]{1,0:T(8,128)}) %reduce-scatter.11.cloned.1.call-update) | async-done | bytes 8208 | tf_op jit(solution)/shard_map/reduce_scatter | solution.py:150
  292.4 81.7 %reduce-scatter.7.cloned.1.call-done = f32[8,512]{1,0:T(8,128)} async-done(((f32[8,8192]{1,0:T(8,128)}), f32[8,512]{1,0:T(8,128)}) %reduce-scatter.7.cloned.1.call-update) | async-done | bytes 16400 | tf_op jit(solution)/shard_map/reduce_scatter | solution.py:149
  (14 shorter events, 0.1 us)
Async XLA Ops:
  7.2 19.2 %copy-start = (bf16[16,8192]{1,0:T(8,128)(2,1)S(1)}, bf16[16,8192]{1,0:T(8,128)(2,1)}, u32[]{:S(2)}) copy-start(bf16[16,8192]{1,0:T(8,128)(2,1)} %param.10) | copy-start | bytes 786436
  7.2 20.3 %copy-start.1 = (f32[4096]{0:T(1024)S(1)}, f32[4096]{0:T(1024)}, u32[]{:S(2)}) copy-start(f32[4096]{0:T(1024)} %param.12) | copy-start | bytes 49156
  9.7 57.8 %all-to-all-start = ((bf16[16,8,8192]{2,1,0:T(8,128)(2,1)}), bf16[16,8,8192]{2,1,0:T(8,128)(2,1)S(1)}, u32[]{:S(2)}, u32[]{:S(2)}) async-start(bf16[16,8,8192]{2,1,0:T(8,128)(2,1)} %stack.2), calls=%async_computation | async-start | bytes 4194304 | tf_op jit(solution)/shard_map/all_to_all | solution.py:139
  18.3 129.0 %reduce-scatter.9.cloned.1.call-start = ((), (), s32[]{:S(2)}) async-start(), calls=%async_computation.7 | async-start | bytes 2228224 | tf_op jit(solution)/shard_map/reduce_scatter | solution.py:146
  88.1 123.9 %reduce-scatter.5.cloned.1.call-start = ((), (), s32[]{:S(2)}) async-start(), calls=%async_computation.5 | async-start | bytes 4456448 | tf_op jit(solution)/shard_map/reduce_scatter | solution.py:145
  125.6 166.8 %reduce-scatter.11.cloned.1.call-start = ((), (), s32[]{:S(2)}) async-start(), calls=%async_computation.8 | async-start | bytes 139264 | tf_op jit(solution)/shard_map/reduce_scatter | solution.py:150
  147.3 226.9 %reduce-scatter.7.cloned.1.call-start = ((), (), s32[]{:S(2)}) async-start(), calls=%async_computation.6 | async-start | bytes 278528 | tf_op jit(solution)/shard_map/reduce_scatter | solution.py:149
Sparse Core Ops, SparseCore 0:
  88.2 58.9 reduce-scatter.8
  149.8 62.1 reduce-scatter.4
  216.1 76.3 reduce-scatter.10
  296.3 77.7 reduce-scatter.6
